TPU v7x, 512 devices: a whole 4x8x8 slice. The times are simulated.
512 devices in a mesh: row: 32 (over x, z), col: 16 (over y, core).
Axes of the slice: x: 4, y: 8, z: 8, core: 2. Of those that a mesh axis runs over, the one named last changes fastest.
Arguments:
- matrix: float32 [14336, 14336], P('row', 'col'), may hold values from -3 to 3
- reflectors: float32 [1, 64, 14336], P(None, None, 'row'), may hold values from -0.09375 to 0.09375
- factors: float32 [1, 64, 64], replicated, may hold values from -0.1 to 2, as said below
Outputs:
- updated: float32 [14336, 14336], P('row', 'col')
- companions: float32 [1, 64, 14336], P(None, None, 'row')
Inputs may be any that keep to these rules, and one draw needn't show every extreme that they name: `factors`: each factor is upper triangular (zero below the diagonal) with diagonal entries between 1 and 2.
All inputs are finite; a program needn't handle non-finite values.
Results may differ from a plain program's by a relative error of at most 0.0001.
Values sent between devices are 32-bit elements; how exact they have to be, the bound alone decides.
No kernel may reach another device: no remote copies, remote signals or barrier semaphores. Data moves between devices by JAX's collectives and lax.ppermute only.
A program may use at most 64 MiB of HBM per device.

v0:
```python
import jax
import jax.numpy as jnp
from jax import lax
from jax.sharding import Mesh
from jax.sharding import PartitionSpec as P


def contract(left_side, right_side, left_dim, right_dim):
    return lax.dot_general(
        left_side,
        right_side,
        (((left_dim,), (right_dim,)), ((), ())),
        precision=lax.Precision.HIGHEST,
        preferred_element_type=jnp.float32,
    )


def gathered_sum(values, axes):
    for axis in axes:
        values = jnp.sum(lax.all_gather(values, axis), axis=0)
    return values


def split_sum(values, axis, split_axis):
    width = values.shape[1] // 2
    mine = jnp.where(lax.axis_index(split_axis) == 0, values[:, :width], values[:, width:])
    total = gathered_sum(mine, (axis,))
    both = lax.all_gather(total, split_axis)
    return jnp.concatenate([both[0], both[1]], axis=1)


def scattered_sum(values, axis, parts):
    chunks = values.reshape((parts, values.shape[0] // parts) + values.shape[1:])
    mine = jnp.sum(lax.all_to_all(chunks, axis, 0, 0, tiled=False), axis=0)
    return lax.all_gather(mine, axis, tiled=True)


def scattered_sum_nested(values, axes, inner_axes=()):
    if not axes:
        return gathered_sum(values, inner_axes)
    parts = lax.axis_size(axes[0])
    chunks = values.reshape((parts, values.shape[0] // parts) + values.shape[1:])
    mine = jnp.sum(lax.all_to_all(chunks, axes[0], 0, 0, tiled=False), axis=0)
    mine = scattered_sum_nested(mine, axes[1:], inner_axes)
    return lax.all_gather(mine, axes[0], tiled=True)


def halves_sum(values, axis):
    width = values.shape[1] // 2
    left = gathered_sum(values[:, :width], (axis,))
    right = gathered_sum(values[:, width:], (axis,))
    return jnp.concatenate([left, right], axis=1)


def column_block_pairs(rows, cols, shift):
    group = rows // cols
    pairs = []
    for r in range(rows):
        for c in range(cols):
            target_row = group * c + (r % group - shift) % group
            pairs.append((r * cols + c, target_row * cols + r // group))
    return pairs


def staged_route(rows, cols):
    sizes = (4, rows // 4, cols // 2, 2)
    if rows % 4 or cols % 2 or sizes[2] % sizes[0]:
        return None
    k = sizes[2] // sizes[0]

    def split(i):
        return (
            i // (sizes[1] * sizes[2] * 2),
            i // (sizes[2] * 2) % sizes[1],
            i // 2 % sizes[2],
            i % 2,
        )

    def join(x, z, y, core):
        return ((x * sizes[1] + z) * sizes[2] + y) * 2 + core

    def hop(i):
        x, z, y, core = split(i)
        return join(y // k, z, k * x + y % k, core)

    return [(i, hop(i)) for i in range(rows * cols)]


def to_column_blocks(values, rows, cols, all_axes, row_index):
    group = rows // cols
    first = staged_route(rows, cols)
    if first is None:
        rounds = [
            lax.ppermute(values, all_axes, column_block_pairs(rows, cols, shift))
            for shift in range(group)
        ]
    else:
        moved = lax.ppermute(values, all_axes, first)
        rounds = []
        for shift in range(group):
            final = dict(column_block_pairs(rows, cols, shift))
            rounds.append(lax.ppermute(moved, all_axes, [(mid, final[i]) for i, mid in first]))
    offset = row_index % group
    blocks = []
    for part in range(group):
        block = rounds[0]
        for shift in range(1, group):
            block = jnp.where((part - offset) % group == shift, rounds[shift], block)
        blocks.append(block)
    return jnp.concatenate(blocks, axis=values.ndim - 1)


def second_hops(moved, rows, cols, all_axes, row_index):
    group = rows // cols
    first = staged_route(rows, cols)
    rounds = []
    for shift in range(group):
        final = dict(column_block_pairs(rows, cols, shift))
        rounds.append(lax.ppermute(moved, all_axes, [(mid, final[i]) for i, mid in first]))
    offset = row_index % group
    blocks = []
    for part in range(group):
        block = rounds[0]
        for shift in range(1, group):
            block = jnp.where((part - offset) % group == shift, rounds[shift], block)
        blocks.append(block)
    return jnp.concatenate(blocks, axis=moved.ndim - 1)


def make_shards(row_axes, col_axes, rows, cols):
    all_axes = tuple(row_axes) + tuple(col_axes)

    def shards(matrix, reflectors, factors):
        current = matrix
        v_rows = reflectors[0]
        factor = factors[0]
        row_index = lax.axis_index(tuple(row_axes))
        chunks = contract(v_rows, current, 1, 0)
        first = row_axes[-1]
        parts = lax.axis_size(first)
        chunks = chunks.reshape((parts, chunks.shape[0] // parts) + chunks.shape[1:])
        mine = jnp.sum(lax.all_to_all(chunks, first, 0, 0, tiled=False), axis=0)
        mine, v_sent = lax.optimization_barrier((mine, v_rows))
        moved = lax.ppermute(v_sent, all_axes, staged_route(rows, cols))
        second = row_axes[-2]
        parts2 = lax.axis_size(second)
        chunks = mine.reshape((parts2, mine.shape[0] // parts2) + mine.shape[1:])
        mine = jnp.sum(lax.all_to_all(chunks, second, 0, 0, tiled=False), axis=0)
        mine = gathered_sum(mine, row_axes[:1])
        mine, moved = lax.optimization_barrier((mine, moved))
        v_cols = second_hops(moved, rows, cols, all_axes, row_index)
        mine = lax.all_gather(mine, second, tiled=True)
        col_sums = lax.all_gather(mine, first, tiled=True)
        partial_value = contract(v_cols, current, 1, 1)
        partial_inner = contract(v_cols, col_sums, 1, 1)
        width = partial_value.shape[1]
        sums = split_sum(
            gathered_sum(jnp.concatenate([partial_value, partial_inner], axis=1), col_axes[1:]),
            col_axes[0],
            col_axes[1],
        )
        row_sums = sums[:, :width]
        inner = sums[:, width:]
        x_rows = contract(factor, row_sums, 0, 0)
        x_cols = contract(factor, col_sums, 0, 0)
        projected = contract(inner, factor, 0, 0)
        mixing = contract(projected, factor, 0, 0)
        w_rows = x_rows - 0.5 * contract(mixing, v_rows, 1, 0)
        w_cols = x_cols - 0.5 * contract(mixing, v_cols, 1, 0)
        current = current - contract(
            jnp.concatenate([v_rows, w_rows], axis=0),
            jnp.concatenate([w_cols, v_cols], axis=0),
            0,
            0,
        )
        return (current, jnp.stack([w_rows]))

    return shards


def solution(mesh):
    rows, cols = (mesh.shape["row"], mesh.shape["col"])
    row_axes, col_axes = (("x", "za", "zb"), ("y", "core"))
    fine = Mesh(mesh.devices.reshape((4, rows // 8, 2, cols // 2, 2)), row_axes + col_axes)
    return jax.shard_map(
        make_shards(row_axes, col_axes, rows, cols),
        mesh=fine,
        in_specs=(P(row_axes, col_axes), P(None, None, row_axes), P()),
        out_specs=(P(row_axes, col_axes), P(None, None, row_axes)),
        check_vma=False,
    )
```

profile of v0, /device:TPU:1, one launch (start us, length us, event | category | flops | bytes accessed | tf_op | source)
XLA Modules:
  0.0 111.3 jit_solution(5235569078798116109)
XLA Ops:
  0.6 0.0 copy-start
  0.6 0.0 copy-start.2
  0.7 2.6 %fusion = f32[2,32,896]{2,1,0:T(8,128)S(1)} fusion(f32[2,32,448]{2,1,0:T(8,128)} %bitcast.36, f32[448,896]{1,0:T(8,128)} %param.3), kind=kOutput, calls=%fused_computation | convolution fusion | flops 308281344 | bytes 1949696 | tf_op jit(solution)/shard_map/dot_general | solution.py:9
  3.2 7.8 %all_to_all.10 = f32[2,32,896]{2,1,0:T(8,128)S(1)} all-to-all(f32[2,32,896]{2,1,0:T(8,128)S(1)} %fusion), channel_id=1, replica_groups=mesh['x'=4,'za'=4,'zb'=2,'y'=8,'core'=2] {'zb'}, dimensions={0} | all-to-all | bytes 458752 | tf_op jit(solution)/shard_map/all_to_all | solution.py:142
  11.1 0.0 copy-start.1
  11.1 0.7 reduce_sum.45
  11.7 9.2 %all-to-all-start.1 = ((f32[4,8,896]{2,1,0:T(8,128)}), f32[4,8,896]{2,1,0:T(8,128)S(1)}, u32[]{:S(2)}, u32[]{:S(2)}) async-start(f32[4,8,896]{2,1,0:T(8,128)} %bitcast.3), calls=%async_computation.1 | async-start | bytes 229376 | tf_op jit(solution)/shard_map/all_to_all | solution.py:148
  20.9 0.0 copy-done.2
  20.9 0.7 collective-permute-start
  21.6 6.5 %all-to-all-done.1 = f32[4,8,896]{2,1,0:T(8,128)S(1)} async-done(((f32[4,8,896]{2,1,0:T(8,128)}), f32[4,8,896]{2,1,0:T(8,128)S(1)}, u32[]{:S(2)}, u32[]{:S(2)}) %all-to-all-start.1) | async-done | bytes 114720 | tf_op jit(solution)/shard_map/all_to_all | solution.py:148
  28.1 10.1 %all-gather = f32[32,896]{1,0:T(8,128)S(1)} all-gather(f32[8,896]{1,0:T(8,128)S(1)} %reduce_sum.46), channel_id=2, replica_groups=mesh['x'=4,'za'=4,'zb'=2,'y'=8,'core'=2] {'x'}, dimensions={0}, use_global_device_ids=true | all-gather | bytes 143360 | tf_op jit(solution)/shard_map/all_gather | solution.py:20
  38.2 0.0 collective-permute-done
  38.2 9.6 %collective-permute-start.2 = (f32[64,448]{1,0:T(8,128)S(1)}, f32[64,448]{1,0:T(8,128)S(1)}, u32[]{:S(2)}, u32[]{:S(2)}) collective-permute-start(f32[64,448]{1,0:T(8,128)S(1)} %collective-permute-done), channel_id=1, source_target_pairs={{0,0},{1,32},{2,64},{3,96},{128,128},{129,160},{130,192},{131,224}... | collective-permute-start | bytes 344072 | tf_op jit(solution)/shard_map/ppermute | solution.py:119
  47.8 1.9 %collective-permute-start.1 = (f32[64,448]{1,0:T(8,128)S(1)}, f32[64,448]{1,0:T(8,128)S(1)}, u32[]{:S(2)}, u32[]{:S(2)}) collective-permute-start(f32[64,448]{1,0:T(8,128)S(1)} %collective-permute-done), channel_id=1, source_target_pairs={{0,16},{1,48},{2,80},{3,112},{128,144},{129,176},{130,208},{131,24... | collective-permute-start | bytes 344072 | tf_op jit(solution)/shard_map/ppermute | solution.py:119
  49.7 17.0 %all_gather.32 = f32[32,896]{1,0:T(8,128)S(1)} all-gather(f32[8,896]{1,0:T(8,128)S(1)} %bitcast_reduce_fusion), channel_id=1, replica_groups=mesh['x'=4,'za'=4,'zb'=2,'y'=8,'core'=2] {'za'}, dimensions={0}, use_global_device_ids=true | all-gather | bytes 143360 | tf_op jit(solution)/shard_map/all_gather | solution.py:152
  66.8 4.3 %all_gather.33 = f32[64,896]{1,0:T(8,128)S(1)} all-gather(f32[32,896]{1,0:T(8,128)S(1)} %all_gather.32), channel_id=1, replica_groups=mesh['x'=4,'za'=4,'zb'=2,'y'=8,'core'=2] {'zb'}, dimensions={0}, use_global_device_ids=true | all-gather | bytes 344064 | tf_op jit(solution)/shard_map/all_gather | solution.py:153
  71.1 0.0 copy-done
  71.1 0.4 convolution_bitcast_fusion
  71.5 0.0 collective-permute-done.2
  71.5 0.0 collective-permute-done.1
  71.5 0.4 fusion.13
  71.9 0.0 copy-done.1
  71.9 1.7 %fusion.14 = f32[64,448]{1,0:T(8,128)S(1)} fusion(f32[448,896]{1,0:T(8,128)S(1)} %copy-done.1, f32[64,448]{1,0:T(8,128)S(1)} %get-tuple-element.11, f32[64,448]{1,0:T(8,128)S(1)} %get-tuple-element.10), kind=kOutput, calls=%fused_computation.22 | convolution fusion | flops 308338688 | bytes 1949696 | tf_op jit(solution)/shard_map/dot_general | solution.py:9
  73.6 0.1 pad_maximum_fusion.3
  73.7 5.9 %all-gather.1 = f32[128,512]{1,0:T(8,128)S(1)} all-gather(f32[64,512]{1,0:T(8,128)S(1)} %pad_maximum_fusion.3), channel_id=3, replica_groups=mesh['x'=4,'za'=4,'zb'=2,'y'=8,'core'=2] {'core'}, dimensions={0}, use_global_device_ids=true | all-gather | bytes 393216 | tf_op jit(solution)/shard_map/all_gather | solution.py:20
  79.6 19.5 %all-gather.2 = f32[512,256]{1,0:T(8,128)S(1)} all-gather(f32[64,256]{1,0:T(8,128)S(1)} %slice_select_fusion), channel_id=4, replica_groups=mesh['x'=4,'za'=4,'zb'=2,'y'=8,'core'=2] {'y'}, dimensions={0}, use_global_device_ids=true | all-gather | bytes 589824 | tf_op jit(solution)/shard_map/all_gather | solution.py:20
  99.2 7.9 %all-gather.3 = f32[128,256]{1,0:T(8,128)S(1)} all-gather(f32[64,256]{1,0:T(8,128)S(1)} %reduce_sum.49), channel_id=5, replica_groups=mesh['x'=4,'za'=4,'zb'=2,'y'=8,'core'=2] {'core'}, dimensions={0}, use_global_device_ids=true | all-gather | bytes 196608 | tf_op jit(solution)/shard_map/all_gather | solution.py:28
  107.1 0.3 fusion.15
  107.4 0.2 fusion.18
  107.7 0.3 convolution_multiply_fusion.1
  107.9 0.4 fusion.2
  108.3 0.3 fusion.3
  108.7 0.0 copy-start.3
  108.7 2.6 %convolution_subtract_fusion = f32[448,896]{1,0:T(8,128)} fusion(f32[448,896]{1,0:T(8,128)S(1)} %copy-done.1, f32[64,448]{1,0:T(8,128)S(1)} %get-tuple-element.11, f32[64,448]{1,0:T(8,128)S(1)} %get-tuple-element.10, f32[64,896]{1,0:T(8,128)S(1)} %fusion.2, f32[64,448]{1,0:T(8,128)S(1)} %fusion.3, f32[64,448]{1,0:T(8,128)S(1)} %bitcast.38), kind=kOutput, calls=%fused_computation.2 | convolution fusion | flops 617250816 | bytes 3899392 | tf_op jit(solution)/shard_map/dot_general | solution.py:9
  111.3 0.0 copy-done.3
  (7 shorter events, 0.1 us)
Async XLA Ops:
  0.6 70.4 %copy-start = (f32[1,64,64]{2,1,0:T(8,128)S(1)}, f32[1,64,64]{2,1,0:T(8,128)}, u32[]{:S(2)}) copy-start(f32[1,64,64]{2,1,0:T(8,128)} %param.5) | copy-start | bytes 49156
  0.6 20.3 %copy-start.2 = (f32[1,64,448]{2,1,0:T(8,128)S(1)}, f32[1,64,448]{2,1,0:T(8,128)}, u32[]{:S(2)}) copy-start(f32[1,64,448]{2,1,0:T(8,128)} %param.4) | copy-start | bytes 344068
  11.1 60.9 %copy-start.1 = (f32[448,896]{1,0:T(8,128)S(1)}, f32[448,896]{1,0:T(8,128)}, u32[]{:S(2)}) copy-start(f32[448,896]{1,0:T(8,128)} %param.3) | copy-start | bytes 4816900
  11.7 16.4 %all-to-all-start.1 = ((f32[4,8,896]{2,1,0:T(8,128)}), f32[4,8,896]{2,1,0:T(8,128)S(1)}, u32[]{:S(2)}, u32[]{:S(2)}) async-start(f32[4,8,896]{2,1,0:T(8,128)} %bitcast.3), calls=%async_computation.1 | async-start | bytes 229376 | tf_op jit(solution)/shard_map/all_to_all | solution.py:148
  20.9 17.3 %collective-permute-start = (f32[64,448]{1,0:T(8,128)S(1)}, f32[64,448]{1,0:T(8,128)S(1)}, u32[]{:S(2)}, u32[]{:S(2)}) collective-permute-start(f32[64,448]{1,0:T(8,128)S(1)} %bitcast.37), channel_id=1, source_target_pairs={{0,0},{1,1},{2,2},{3,3},{4,128},{5,129},{6,130},{7,131},{8,256},{9... | collective-permute-start | bytes 344072 | tf_op jit(solution)/shard_map/ppermute | solution.py:144
  38.2 33.2 %collective-permute-start.2 = (f32[64,448]{1,0:T(8,128)S(1)}, f32[64,448]{1,0:T(8,128)S(1)}, u32[]{:S(2)}, u32[]{:S(2)}) collective-permute-start(f32[64,448]{1,0:T(8,128)S(1)} %collective-permute-done), channel_id=1, source_target_pairs={{0,0},{1,32},{2,64},{3,96},{128,128},{129,160},{130,192},{131,224}... | collective-permute-start | bytes 344072 | tf_op jit(solution)/shard_map/ppermute | solution.py:119
  47.8 23.7 %collective-permute-start.1 = (f32[64,448]{1,0:T(8,128)S(1)}, f32[64,448]{1,0:T(8,128)S(1)}, u32[]{:S(2)}, u32[]{:S(2)}) collective-permute-start(f32[64,448]{1,0:T(8,128)S(1)} %collective-permute-done), channel_id=1, source_target_pairs={{0,16},{1,48},{2,80},{3,112},{128,144},{129,176},{130,208},{131,24... | collective-permute-start | bytes 344072 | tf_op jit(solution)/shard_map/ppermute | solution.py:119
  108.7 2.7 %copy-start.3 = (f32[64,448]{1,0:T(8,128)}, f32[64,448]{1,0:T(8,128)S(1)}, u32[]{:S(2)}) copy-start(f32[64,448]{1,0:T(8,128)S(1)} %fusion.3) | copy-start | bytes 344068
where the time goes:
time: 112 us; the launch traced here: 111 us
  blocking collectives  72.6 us (65%)
  starting transfers between devices  21.4 us (19%)
  matrix products  9.15 us (8%)
  waiting for transfers between devices  6.48 us (6%)
    all_gather x3, blocking collectives, gathered_sum(): values = jnp.sum(lax.all_gather(values, axis), axis=0)  35.6 us
    all_gather x1, blocking collectives, shards(): mine = lax.all_gather(mine, second, tiled=True)  17 us
    ppermute x2, starting transfers between devices, second_hops(): lax.ppermute(moved, all_axes, [(mid, final[i]) for i, mid in first])  11.5 us
    all_to_all x1, starting transfers between devices, shards(): mine = jnp.sum(lax.all_to_all(chunks, second, 0, 0, tiled=False), axis=0)  9.22 us
    dot_general x10, matrix products, contract(): lax.dot_general(left_side, right_side, (((left_dim,), (right_dim,)), ((),...  9.15 us
    all_gather x1, blocking collectives, split_sum(): both = lax.all_gather(total, split_axis)  7.91 us
    all_to_all x1, blocking collectives, shards(): mine = jnp.sum(lax.all_to_all(chunks, first, 0, 0, tiled=False), axis=0)  7.84 us
    all_to_all x1, waiting for transfers between devices, shards(): mine = jnp.sum(lax.all_to_all(chunks, second, 0, 0, tiled=False), axis=0)  6.47 us
  transfers between devices with their start and end apart: 4, of which 1 were waited for; matrix products, arithmetic and copies ran while one was open for 0% of the time, Pallas kernels for 0%

commit v1 on v0

--- a/solution.py
+++ b/solution.py
@@ -3,6 +3,13 @@
 from jax import lax
 from jax.sharding import Mesh
 from jax.sharding import PartitionSpec as P
+
+
+def exchange_gather(shard, axis, along):
+    size = lax.axis_size(axis)
+    blocks = jnp.stack([shard for _ in range(size)])
+    blocks = lax.all_to_all(blocks, axis, split_axis=0, concat_axis=0)
+    return jnp.concatenate(blocks, axis=along)
 
 
 def contract(left_side, right_side, left_dim, right_dim):
@@ -150,7 +157,7 @@
         mine, moved = lax.optimization_barrier((mine, moved))
         v_cols = second_hops(moved, rows, cols, all_axes, row_index)
         mine = lax.all_gather(mine, second, tiled=True)
-        col_sums = lax.all_gather(mine, first, tiled=True)
+        col_sums = exchange_gather(mine, first, 0)
         partial_value = contract(v_cols, current, 1, 1)
         partial_inner = contract(v_cols, col_sums, 1, 1)
         width = partial_value.shape[1]

time: 112 us -> 114 us (1.018)
  blocking collectives: 72.6 us -> 68.5 us
  starting transfers between devices: 21.4 us -> 24.8 us
  waiting for transfers between devices: 6.48 us -> 8.6 us
    all_gather x1 -> x0, blocking collectives: 4.31 us -> none  [shards(): col_sums = lax.all_gather(mine, first, tiled=True)]
    all_to_all x0 -> x1, starting transfers between devices: none -> 3.44 us  [exchange_gather(): blocks = lax.all_to_all(blocks, axis, split_axis=0, concat_axis=0)]
    all_to_all x0 -> x1, waiting for transfers between devices: none -> 2.12 us  [exchange_gather(): blocks = lax.all_to_all(blocks, axis, split_axis=0, concat_axis=0)]
  transfers between devices with their start and end apart: 4 -> 5, of which waited for: 1 -> 2; matrix products, arithmetic and copies ran while one was open for 0% -> 2% of each run, Pallas kernels for 0% -> 0%
where the time goes in v1:
time: 114 us; the launch traced here: 113 us
  blocking collectives  68.5 us (60%)
  starting transfers between devices  24.8 us (22%)
  matrix products  9.15 us (8%)
  waiting for transfers between devices  8.6 us (8%)
  other arithmetic  1.55 us (1%)
    all_gather x3, blocking collectives, gathered_sum(): values = jnp.sum(lax.all_gather(values, axis), axis=0)  35.6 us
    all_gather x1, blocking collectives, shards(): mine = lax.all_gather(mine, second, tiled=True)  17 us
    ppermute x2, starting transfers between devices, second_hops(): lax.ppermute(moved, all_axes, [(mid, final[i]) for i, mid in first])  11.5 us
    all_to_all x1, starting transfers between devices, shards(): mine = jnp.sum(lax.all_to_all(chunks, second, 0, 0, tiled=False), axis=0)  9.22 us
    dot_general x10, matrix products, contract(): lax.dot_general(left_side, right_side, (((left_dim,), (right_dim,)), ((),...  9.15 us
    all_to_all x1, blocking collectives, shards(): mine = jnp.sum(lax.all_to_all(chunks, first, 0, 0, tiled=False), axis=0)  7.97 us
    all_gather x1, blocking collectives, split_sum(): both = lax.all_gather(total, split_axis)  7.92 us
    all_to_all x1, waiting for transfers between devices, shards(): mine = jnp.sum(lax.all_to_all(chunks, second, 0, 0, tiled=False), axis=0)  6.47 us
  transfers between devices with their start and end apart: 5, of which 2 were waited for; matrix products, arithmetic and copies ran while one was open for 2% of the time, Pallas kernels for 0%

profile of v1, /device:TPU:1, one launch (start us, length us, event | category | flops | bytes accessed | tf_op | source)
XLA Modules:
  0.0 113.4 jit_solution(12588668893226015279)
XLA Ops:
  0.6 0.0 copy-start
  0.6 0.0 copy-start.2
  0.7 2.6 %fusion = f32[2,32,896]{2,1,0:T(8,128)S(1)} fusion(f32[2,32,448]{2,1,0:T(8,128)} %bitcast.40, f32[448,896]{1,0:T(8,128)} %param.3), kind=kOutput, calls=%fused_computation | convolution fusion | flops 308281344 | bytes 1949696 | tf_op jit(solution)/shard_map/dot_general | solution.py:16
  3.2 0.0 copy-start.1
  3.2 8.0 %all_to_all.15 = f32[2,32,896]{2,1,0:T(8,128)S(1)} all-to-all(f32[2,32,896]{2,1,0:T(8,128)S(1)} %fusion), channel_id=1, replica_groups=mesh['x'=4,'za'=4,'zb'=2,'y'=8,'core'=2] {'zb'}, dimensions={0} | all-to-all | bytes 458752 | tf_op jit(solution)/shard_map/all_to_all | solution.py:149
  11.2 0.7 reduce_sum.45
  11.9 9.2 %all-to-all-start.1 = ((f32[4,8,896]{2,1,0:T(8,128)}), f32[4,8,896]{2,1,0:T(8,128)S(1)}, u32[]{:S(2)}, u32[]{:S(2)}) async-start(f32[4,8,896]{2,1,0:T(8,128)} %bitcast.3), calls=%async_computation.1 | async-start | bytes 229376 | tf_op jit(solution)/shard_map/all_to_all | solution.py:155
  21.1 0.0 copy-done.2
  21.1 0.7 collective-permute-start
  21.8 6.5 %all-to-all-done.1 = f32[4,8,896]{2,1,0:T(8,128)S(1)} async-done(((f32[4,8,896]{2,1,0:T(8,128)}), f32[4,8,896]{2,1,0:T(8,128)S(1)}, u32[]{:S(2)}, u32[]{:S(2)}) %all-to-all-start.1) | async-done | bytes 114720 | tf_op jit(solution)/shard_map/all_to_all | solution.py:155
  28.2 10.1 %all-gather = f32[32,896]{1,0:T(8,128)S(1)} all-gather(f32[8,896]{1,0:T(8,128)S(1)} %reduce_sum.46), channel_id=2, replica_groups=mesh['x'=4,'za'=4,'zb'=2,'y'=8,'core'=2] {'x'}, dimensions={0}, use_global_device_ids=true | all-gather | bytes 143360 | tf_op jit(solution)/shard_map/all_gather | solution.py:27
  38.4 0.0 collective-permute-done
  38.4 9.6 %collective-permute-start.2 = (f32[64,448]{1,0:T(8,128)S(1)}, f32[64,448]{1,0:T(8,128)S(1)}, u32[]{:S(2)}, u32[]{:S(2)}) collective-permute-start(f32[64,448]{1,0:T(8,128)S(1)} %collective-permute-done), channel_id=1, source_target_pairs={{0,0},{1,32},{2,64},{3,96},{128,128},{129,160},{130,192},{131,224}... | collective-permute-start | bytes 344072 | tf_op jit(solution)/shard_map/ppermute | solution.py:126
  48.0 1.9 %collective-permute-start.1 = (f32[64,448]{1,0:T(8,128)S(1)}, f32[64,448]{1,0:T(8,128)S(1)}, u32[]{:S(2)}, u32[]{:S(2)}) collective-permute-start(f32[64,448]{1,0:T(8,128)S(1)} %collective-permute-done), channel_id=1, source_target_pairs={{0,16},{1,48},{2,80},{3,112},{128,144},{129,176},{130,208},{131,24... | collective-permute-start | bytes 344072 | tf_op jit(solution)/shard_map/ppermute | solution.py:126
  49.9 17.0 %all_gather.29 = f32[32,896]{1,0:T(8,128)S(1)} all-gather(f32[8,896]{1,0:T(8,128)S(1)} %bitcast_reduce_fusion), channel_id=1, replica_groups=mesh['x'=4,'za'=4,'zb'=2,'y'=8,'core'=2] {'za'}, dimensions={0}, use_global_device_ids=true | all-gather | bytes 143360 | tf_op jit(solution)/shard_map/all_gather | solution.py:159
  66.9 0.7 pad_maximum_fusion.1
  67.6 3.4 %all-to-all-start.2 = ((f32[2,32,896]{2,1,0:T(8,128)}), f32[2,32,896]{2,1,0:T(8,128)S(1)}, u32[]{:S(2)}, u32[]{:S(2)}) async-start(f32[2,32,896]{2,1,0:T(8,128)} %pad_maximum_fusion.1), calls=%async_computation.2 | async-start | bytes 458752 | tf_op jit(solution)/shard_map/all_to_all | solution.py:11
  71.0 0.0 collective-permute-done.2
  71.1 0.0 collective-permute-done.1
  71.1 0.0 copy-done.1
  71.1 1.7 %fusion.14 = f32[64,448]{1,0:T(8,128)S(1)} fusion(f32[448,896]{1,0:T(8,128)S(1)} %copy-done.1, f32[64,448]{1,0:T(8,128)S(1)} %get-tuple-element.11, f32[64,448]{1,0:T(8,128)S(1)} %get-tuple-element.10), kind=kOutput, calls=%fused_computation.23 | convolution fusion | flops 308338688 | bytes 1949696 | tf_op jit(solution)/shard_map/dot_general | solution.py:16
  72.8 2.1 %all-to-all-done.2 = f32[2,32,896]{2,1,0:T(8,128)S(1)} async-done(((f32[2,32,896]{2,1,0:T(8,128)}), f32[2,32,896]{2,1,0:T(8,128)S(1)}, u32[]{:S(2)}, u32[]{:S(2)}) %all-to-all-start.2) | async-done | bytes 229408 | tf_op jit(solution)/shard_map/all_to_all | solution.py:11
  74.9 0.4 fusion.13
  75.3 0.0 copy-done
  75.3 0.4 convolution_bitcast_fusion
  75.7 0.1 pad_maximum_fusion.4
  75.8 5.9 %all-gather.1 = f32[128,512]{1,0:T(8,128)S(1)} all-gather(f32[64,512]{1,0:T(8,128)S(1)} %pad_maximum_fusion.4), channel_id=3, replica_groups=mesh['x'=4,'za'=4,'zb'=2,'y'=8,'core'=2] {'core'}, dimensions={0}, use_global_device_ids=true | all-gather | bytes 393216 | tf_op jit(solution)/shard_map/all_gather | solution.py:27
  81.7 19.5 %all-gather.2 = f32[512,256]{1,0:T(8,128)S(1)} all-gather(f32[64,256]{1,0:T(8,128)S(1)} %slice_select_fusion), channel_id=4, replica_groups=mesh['x'=4,'za'=4,'zb'=2,'y'=8,'core'=2] {'y'}, dimensions={0}, use_global_device_ids=true | all-gather | bytes 589824 | tf_op jit(solution)/shard_map/all_gather | solution.py:27
  101.3 7.9 %all-gather.3 = f32[128,256]{1,0:T(8,128)S(1)} all-gather(f32[64,256]{1,0:T(8,128)S(1)} %reduce_sum.49), channel_id=5, replica_groups=mesh['x'=4,'za'=4,'zb'=2,'y'=8,'core'=2] {'core'}, dimensions={0}, use_global_device_ids=true | all-gather | bytes 196608 | tf_op jit(solution)/shard_map/all_gather | solution.py:35
  109.2 0.3 fusion.15
  109.5 0.2 fusion.18
  109.8 0.3 convolution_multiply_fusion.1
  110.0 0.4 fusion.2
  110.4 0.3 fusion.3
  110.8 0.0 copy-start.3
  110.8 2.6 %convolution_subtract_fusion = f32[448,896]{1,0:T(8,128)} fusion(f32[448,896]{1,0:T(8,128)S(1)} %copy-done.1, f32[64,448]{1,0:T(8,128)S(1)} %get-tuple-element.11, f32[64,448]{1,0:T(8,128)S(1)} %get-tuple-element.10, f32[64,896]{1,0:T(8,128)S(1)} %fusion.2, f32[64,448]{1,0:T(8,128)S(1)} %fusion.3, f32[64,448]{1,0:T(8,128)S(1)} %bitcast.42), kind=kOutput, calls=%fused_computation.2 | convolution fusion | flops 617250816 | bytes 3899392 | tf_op jit(solution)/shard_map/dot_general | solution.py:16
  113.4 0.0 copy-done.3
  (7 shorter events, 0.1 us)
Async XLA Ops:
  0.6 74.7 %copy-start = (f32[1,64,64]{2,1,0:T(8,128)S(1)}, f32[1,64,64]{2,1,0:T(8,128)}, u32[]{:S(2)}) copy-start(f32[1,64,64]{2,1,0:T(8,128)} %param.5) | copy-start | bytes 49156
  0.6 20.4 %copy-start.2 = (f32[1,64,448]{2,1,0:T(8,128)S(1)}, f32[1,64,448]{2,1,0:T(8,128)}, u32[]{:S(2)}) copy-start(f32[1,64,448]{2,1,0:T(8,128)} %param.4) | copy-start | bytes 344068
  3.2 67.9 %copy-start.1 = (f32[448,896]{1,0:T(8,128)S(1)}, f32[448,896]{1,0:T(8,128)}, u32[]{:S(2)}) copy-start(f32[448,896]{1,0:T(8,128)} %param.3) | copy-start | bytes 4816900
  11.9 16.4 %all-to-all-start.1 = ((f32[4,8,896]{2,1,0:T(8,128)}), f32[4,8,896]{2,1,0:T(8,128)S(1)}, u32[]{:S(2)}, u32[]{:S(2)}) async-start(f32[4,8,896]{2,1,0:T(8,128)} %bitcast.3), calls=%async_computation.1 | async-start | bytes 229376 | tf_op jit(solution)/shard_map/all_to_all | solution.py:155
  21.1 17.3 %collective-permute-start = (f32[64,448]{1,0:T(8,128)S(1)}, f32[64,448]{1,0:T(8,128)S(1)}, u32[]{:S(2)}, u32[]{:S(2)}) collective-permute-start(f32[64,448]{1,0:T(8,128)S(1)} %bitcast.41), channel_id=1, source_target_pairs={{0,0},{1,1},{2,2},{3,3},{4,128},{5,129},{6,130},{7,131},{8,256},{9... | collective-permute-start | bytes 344072 | tf_op jit(solution)/shard_map/ppermute | solution.py:151
  38.4 32.7 %collective-permute-start.2 = (f32[64,448]{1,0:T(8,128)S(1)}, f32[64,448]{1,0:T(8,128)S(1)}, u32[]{:S(2)}, u32[]{:S(2)}) collective-permute-start(f32[64,448]{1,0:T(8,128)S(1)} %collective-permute-done), channel_id=1, source_target_pairs={{0,0},{1,32},{2,64},{3,96},{128,128},{129,160},{130,192},{131,224}... | collective-permute-start | bytes 344072 | tf_op jit(solution)/shard_map/ppermute | solution.py:126
  48.0 23.1 %collective-permute-start.1 = (f32[64,448]{1,0:T(8,128)S(1)}, f32[64,448]{1,0:T(8,128)S(1)}, u32[]{:S(2)}, u32[]{:S(2)}) collective-permute-start(f32[64,448]{1,0:T(8,128)S(1)} %collective-permute-done), channel_id=1, source_target_pairs={{0,16},{1,48},{2,80},{3,112},{128,144},{129,176},{130,208},{131,24... | collective-permute-start | bytes 344072 | tf_op jit(solution)/shard_map/ppermute | solution.py:126
  67.6 7.3 %all-to-all-start.2 = ((f32[2,32,896]{2,1,0:T(8,128)}), f32[2,32,896]{2,1,0:T(8,128)S(1)}, u32[]{:S(2)}, u32[]{:S(2)}) async-start(f32[2,32,896]{2,1,0:T(8,128)} %pad_maximum_fusion.1), calls=%async_computation.2 | async-start | bytes 458752 | tf_op jit(solution)/shard_map/all_to_all | solution.py:11
  110.8 2.7 %copy-start.3 = (f32[64,448]{1,0:T(8,128)}, f32[64,448]{1,0:T(8,128)S(1)}, u32[]{:S(2)}) copy-start(f32[64,448]{1,0:T(8,128)S(1)} %fusion.3) | copy-start | bytes 344068
